TPU v7x, 256 devices: a whole 4x4x8 slice. The times are simulated.
256 devices in a mesh: seq: 64 (over x, z, core), ch: 4 (over y).
Axes of the slice: x: 4, y: 4, z: 8, core: 2. Of those that a mesh axis runs over, the one named last changes fastest.
Arguments:
- inputs: bfloat16 [8192, 4096], P('seq'), may hold values from -6 to 6
- norm_gain: float32 [4096], replicated, may hold values from 0.1 to 1.9
- in_weight: bfloat16 [4096, 3, 1024], P('seq', None, 'ch'), may hold values from -0.09375 to 0.09375
- short_filter: float32 [3, 3, 1024], P(None, None, 'ch'), may hold values from -4 to 4
- long_filter: float32 [8192, 1024], P('seq', 'ch'), may hold values from -2.2 to 2.2
- conv_bias: float32 [1024], P('ch'), may hold values from -4 to 4
- out_weight: bfloat16 [1024, 4096], P('ch', 'seq'), may hold values from -0.1875 to 0.1875
- out_grad: bfloat16 [8192, 4096], P('seq'), may hold values from -6 to 6
Outputs:
- block_out: bfloat16 [8192, 4096], P('seq', 'ch')
- in_grad: bfloat16 [8192, 4096], P('seq')
- filter_grad: float32 [8192, 1024], P('seq', 'ch')
All inputs are finite; a program needn't handle non-finite values.
Results may differ from a plain program's by a relative error of at most 0.013.
Values may be sent and summed in bfloat16 or wider, within the bound.
No kernel may reach another device: no remote copies, remote signals or barrier semaphores. Data moves between devices by JAX's collectives and lax.ppermute only.
A program may use at most 64 MiB of HBM per device.

v0:
```python
import math
import jax
import jax.numpy as jnp
from jax import lax
from jax.sharding import PartitionSpec as P

epsilon = 1e-05
highest = lax.Precision.HIGHEST


def passed_along(block, axis, distance):
    devices = range(lax.axis_size(axis))
    route = [(i - distance, i) for i in devices if i - distance in devices]
    return lax.ppermute(block, axis, route)


def to_columns(signals):
    return lax.all_to_all(signals, "seq", split_axis=1, concat_axis=2, tiled=True)


def to_rows(signals):
    return lax.all_to_all(signals, "seq", split_axis=2, concat_axis=1, tiled=True)


def turn_table(rows, cols, period, sign):
    turns = jnp.arange(rows, dtype=jnp.int32)[:, None] * jnp.arange(cols, dtype=jnp.int32)[None, :]
    phases = sign * 2.0 * math.pi / period * (turns % period).astype(jnp.float32)
    return (jnp.cos(phases), jnp.sin(phases))


def fft_sizes(seq_total):
    total = 2 * seq_total
    inner = 1
    while inner * inner < total:
        inner *= 2
    return (total // inner, inner)


def forward_dft(signals):
    count, chans, seq_total = signals.shape
    outer, inner = fft_sizes(seq_total)
    grid = signals.reshape(count, chans, outer // 2, inner)
    cos_out, sin_out = turn_table(outer, outer // 2, outer, 1.0)
    first_real = jnp.einsum("kn,ucnm->uckm", cos_out, grid, precision=highest)
    first_imag = -jnp.einsum("kn,ucnm->uckm", sin_out, grid, precision=highest)
    cos_tw, sin_tw = turn_table(outer, inner, outer * inner, 1.0)
    turned_real = first_real * cos_tw + first_imag * sin_tw
    turned_imag = first_imag * cos_tw - first_real * sin_tw
    cos_in, sin_in = turn_table(inner, inner, inner, 1.0)
    spec_real = jnp.einsum("uckm,mj->uckj", turned_real, cos_in, precision=highest) + jnp.einsum(
        "uckm,mj->uckj", turned_imag, sin_in, precision=highest
    )
    spec_imag = jnp.einsum("uckm,mj->uckj", turned_imag, cos_in, precision=highest) - jnp.einsum(
        "uckm,mj->uckj", turned_real, sin_in, precision=highest
    )
    return (spec_real, spec_imag)


def inverse_dft(spec_real, spec_imag):
    count, chans, outer, inner = spec_real.shape
    cos_in, sin_in = turn_table(inner, inner, inner, 1.0)
    back_real = jnp.einsum("uckj,jm->uckm", spec_real, cos_in, precision=highest) - jnp.einsum(
        "uckj,jm->uckm", spec_imag, sin_in, precision=highest
    )
    back_imag = jnp.einsum("uckj,jm->uckm", spec_imag, cos_in, precision=highest) + jnp.einsum(
        "uckj,jm->uckm", spec_real, sin_in, precision=highest
    )
    cos_tw, sin_tw = turn_table(outer, inner, outer * inner, 1.0)
    turned_real = back_real * cos_tw - back_imag * sin_tw
    turned_imag = back_imag * cos_tw + back_real * sin_tw
    cos_out, sin_out = turn_table(outer, outer // 2, outer, 1.0)
    grid = jnp.einsum("kn,uckm->ucnm", cos_out, turned_real, precision=highest) - jnp.einsum(
        "kn,uckm->ucnm", sin_out, turned_imag, precision=highest
    )
    return grid.reshape(count, chans, outer * inner // 2) / float(outer * inner)


def per_device(
    inputs, norm_gain, in_weight, short_filter, long_filter, conv_bias, out_weight, out_grad
):
    local_rows = inputs.shape[0]
    model_width = inputs.shape[1]
    slab_width = long_filter.shape[1]
    taps = short_filter.shape[1]
    wide_inputs = inputs.astype(jnp.float32)
    inv_rms = lax.rsqrt(jnp.mean(wide_inputs * wide_inputs, axis=1, keepdims=True) + epsilon)
    normed = (wide_inputs * inv_rms * norm_gain).astype(jnp.bfloat16)
    in_panel, out_panel = (
        lax.all_gather(in_weight, "seq", axis=0, tiled=True),
        lax.all_gather(out_weight, "seq", axis=1, tiled=True),
    )
    in_flat = in_panel.reshape(model_width, 3 * slab_width)
    projected = jnp.dot(normed, in_flat, preferred_element_type=jnp.float32)
    projected = projected.astype(jnp.bfloat16).reshape(local_rows, 3, slab_width)
    upper_rim = passed_along(projected[local_rows - (taps - 1) :], "seq", 1)
    extended = jnp.concatenate([upper_rim, projected], 0).astype(jnp.float32)
    mixed = jnp.zeros((local_rows, 3, slab_width), jnp.float32)
    for offset in range(taps):
        begin = taps - 1 - offset
        mixed = mixed + short_filter[:, offset, :][None] * extended[begin : begin + local_rows]
    query_br = mixed[:, 0]
    key_br = mixed[:, 1]
    value_br = mixed[:, 2]
    product = key_br * value_br
    gate_grad = jnp.dot(out_grad, out_panel.T, preferred_element_type=jnp.float32)
    carried = gate_grad * query_br
    columns = to_columns(jnp.stack([product, long_filter, carried]).transpose(0, 2, 1))
    all_real, all_imag = forward_dft(columns)
    sig_real, filt_real, grad_real = (all_real[0], all_real[1], all_real[2])
    sig_imag, filt_imag, grad_imag = (all_imag[0], all_imag[1], all_imag[2])
    conv_real = sig_real * filt_real - sig_imag * filt_imag
    conv_imag = sig_real * filt_imag + sig_imag * filt_real
    back_real = grad_real * filt_real + grad_imag * filt_imag
    back_imag = grad_imag * filt_real - grad_real * filt_imag
    pair_real = grad_real * sig_real + grad_imag * sig_imag
    pair_imag = grad_imag * sig_real - grad_real * sig_imag
    outs = inverse_dft(
        jnp.stack([conv_real, back_real, pair_real]), jnp.stack([conv_imag, back_imag, pair_imag])
    )
    returned = to_rows(outs).transpose(0, 2, 1)
    conv_out = returned[0]
    back_conv = returned[1]
    filter_grad = returned[2] * float(local_rows * lax.axis_size("seq")) ** (-0.5)
    biased = conv_out + conv_bias * product
    gated = (query_br * biased).astype(jnp.bfloat16)
    partial_out = jnp.dot(gated, out_panel, preferred_element_type=jnp.float32)
    summed = lax.psum_scatter(
        partial_out.astype(jnp.bfloat16), "ch", scatter_dimension=1, tiled=True
    ).astype(jnp.float32)
    share = summed.shape[1]
    residual = lax.dynamic_slice_in_dim(wide_inputs, lax.axis_index("ch") * share, share, 1)
    block_out = (residual + summed).astype(jnp.bfloat16)
    source_grad = back_conv + conv_bias * carried
    mixed_grad = jnp.stack([gate_grad * biased, source_grad * value_br, source_grad * key_br], 1)
    lower_rim = passed_along(mixed_grad[: taps - 1], "seq", -1)
    extended_back = jnp.concatenate([mixed_grad, lower_rim], 0)
    proj_grad = jnp.zeros((local_rows, 3, slab_width), jnp.float32)
    for offset in range(taps):
        proj_grad = (
            proj_grad
            + short_filter[:, offset, :][None] * extended_back[offset : offset + local_rows]
        )
    proj_grad = proj_grad.astype(jnp.bfloat16).reshape(local_rows, 3 * slab_width)
    partial_grad = jnp.dot(proj_grad, in_flat.T, preferred_element_type=jnp.float32)
    norm_grad = lax.psum(partial_grad, "ch")
    weighted = norm_grad * norm_gain
    inner_term = jnp.mean(weighted * wide_inputs, axis=1, keepdims=True)
    in_grad = (
        out_grad.astype(jnp.float32) + weighted * inv_rms - wide_inputs * inv_rms**3 * inner_term
    ).astype(jnp.bfloat16)
    return (block_out, in_grad, filter_grad)


def solution(mesh):
    return jax.shard_map(
        per_device,
        mesh=mesh,
        in_specs=(
            P("seq", None),
            P(),
            P("seq", None, "ch"),
            P(None, None, "ch"),
            P("seq", "ch"),
            P("ch"),
            P("ch", "seq"),
            P("seq", None),
        ),
        out_specs=(P("seq", "ch"), P("seq", None), P("seq", "ch")),
        check_vma=False,
    )
```

profile of v0, /device:TPU:1, one launch (start us, length us, event | category | flops | bytes accessed | tf_op | source)
XLA Modules:
  0.0 393.4 jit_solution(6677568835043596494)
XLA Ops:
  7.2 0.0 all-gather.3.cloned.1.call-start
  7.2 0.7 all-gather.3.cloned.1.call-update
  7.9 0.0 all-gather.5.cloned.1.call-start
  7.9 0.7 all-gather.5.cloned.1.call-update
  8.6 0.8 fusion.142
  9.5 1.5 multiply_reduce_fusion.1
  11.0 0.6 multiply_multiply_fusion
  11.6 83.9 %all-gather.3.cloned.1.call-done = bf16[4096,3,256]{2,0,1:T(8,128)(2,1)} async-done(((bf16[64,3,256]{2,0,1:T(8,128)(2,1)}), bf16[4096,3,256]{2,0,1:T(8,128)(2,1)}) %all-gather.3.cloned.1.call-update) | async-done | bytes 6291472 | tf_op jit(solution)/shard_map/all_gather | solution.py:89
  95.5 8.7 %copy.46 = bf16[4096,3,256]{0,2,1:T(8,128)(2,1)} copy(bf16[4096,3,256]{2,0,1:T(8,128)(2,1)} %all-gather.3.cloned.1.call-done) | data formatting | bytes 12582912 | tf_op jit(solution)/shard_map/all_gather | solution.py:89
  104.2 5.1 %convolution_convert_fusion.1 = bf16[128,768]{1,0:T(8,128)(2,1)S(1)} fusion(bf16[4096,768]{0,1:T(8,128)(2,1)} %bitcast.127, bf16[128,4096]{1,0:T(8,128)(2,1)S(1)} %copy-done, f32[4096]{0:T(1024)S(1)} %copy-done.9, f32[128]{0:T(128)S(1)} %get-tuple-element.19), kind=kOutput, calls=%fused_computation.16 | convolution fusion | flops 807501824 | bytes 7553536 | tf_op jit(solution)/shard_map/dot_general | solution.py:93
  109.3 2.7 collective-permute-start
  112.1 60.2 %all-gather.5.cloned.1.call-done = bf16[256,4096]{0,1:T(8,128)(2,1)} async-done(((bf16[256,64]{0,1:T(8,128)(2,1)}), bf16[256,4096]{0,1:T(8,128)(2,1)}) %all-gather.5.cloned.1.call-update) | async-done | bytes 2097168 | tf_op jit(solution)/shard_map/all_gather | solution.py:90
  172.3 2.0 fusion.143
  174.4 0.2 copy.48
  174.6 0.2 copy.49
  174.8 0.1 fusion.17
  175.0 0.4 copy-done.8
  175.4 1.0 copy.50
  176.4 6.6 %all-to-all-start = ((f32[3,256,128]{2,0,1:T(4,128)}), f32[3,256,128]{2,0,1:T(4,128)S(1)}, u32[]{:S(2)}, u32[]{:S(2)}) async-start(f32[3,256,128]{2,0,1:T(4,128)} %copy.50), calls=%async_computation | async-start | bytes 1048576 | tf_op jit(solution)/shard_map/all_to_all | solution.py:18
  183.0 0.2 reduce-scatter.2.cloned.1.call-start
  183.2 0.3 fusion.78
  183.5 0.1 copy.53
  183.6 0.3 fusion.77
  183.8 0.1 copy.54
  183.9 16.3 %all-to-all-done = f32[3,256,128]{2,0,1:T(4,128)S(1)} async-done(((f32[3,256,128]{2,0,1:T(4,128)}), f32[3,256,128]{2,0,1:T(4,128)S(1)}, u32[]{:S(2)}, u32[]{:S(2)}) %all-to-all-start) | async-done | bytes 393248 | tf_op jit(solution)/shard_map/all_to_all | solution.py:18
  200.3 1.5 convolution_bitcast_fusion.1
  201.8 1.5 fusion
  203.3 1.6 fusion.31
  204.9 1.6 fusion.32
  206.5 1.6 convolution_add_fusion.1
  208.1 1.6 convolution_subtract_fusion.1
  209.7 0.1 multiply_add_fusion.3
  209.8 0.1 multiply_subtract_fusion.3
  209.9 1.1 fusion.13
  211.0 1.3 fusion.12
  212.4 1.1 convolution_subtract_fusion
  213.5 1.1 convolution_add_fusion
  214.6 1.2 fusion.8
  215.8 1.2 fusion.2
  217.0 8.6 %copy.85 = f32[3,4,64,128]{1,0,3,2:T(4,128)} copy(f32[3,4,64,128]{3,2,1,0:T(8,128)S(1)} %fusion.2) | data formatting | bytes 786432 | tf_op jit(solution)/shard_map/div | solution.py:75
  225.6 16.0 %reshape.105 = f32[64,1,1536]{2,1,0:T(1,128)S(1)} reshape(f32[8192,3,4]{2,1,0:T(4,128)} %bitcast.125) | data formatting | bytes 786432
  241.6 20.6 %all_to_all.33 = f32[64,1,1536]{2,1,0:T(1,128)S(1)} all-to-all(f32[64,1,1536]{2,1,0:T(1,128)S(1)} %reshape.105), channel_id=1, replica_groups=mesh['seq'=64,'ch'=4] {'seq'}, dimensions={0} | all-to-all | bytes 786432 | tf_op jit(solution)/shard_map/all_to_all | solution.py:22
  262.3 0.5 broadcast.224
  262.8 1.6 reduce
  264.4 11.6 %reshape.106 = f32[8192,3,4]{2,1,0:T(4,128)} reshape(f32[64,1536]{1,0:T(8,128)S(1)} %reduce) | data formatting | bytes 786432
  275.9 10.1 %copy.86 = f32[3,4,64,128]{3,2,1,0:T(8,128)} copy(f32[3,4,64,128]{1,0,3,2:T(4,128)} %bitcast.126) | data formatting | bytes 786432 | tf_op jit(solution)/shard_map/all_to_all | solution.py:22
  286.0 2.2 copy.67
  288.1 1.9 copy.68
  290.0 1.8 fusion.37
  291.9 1.8 convolution_convert_fusion
  293.7 0.0 all-reduce.2.cloned.1.call-start
  293.7 1.0 fusion.38
  294.7 1.0 pad_maximum_fusion.7
  295.7 2.6 collective-permute-start.1
  298.3 2.4 collective-permute-done.1
  300.7 6.4 %convolution_bitcast_fusion = f32[128,4096]{1,0:T(8,128)} fusion(bf16[4096,3,256]{2,0,1:T(8,128)(2,1)} %all-gather.3.cloned.1.call-done, f32[130,3,256]{2,0,1:T(8,128)S(1)} %pad_maximum_fusion.6, f32[3,256]{1,0:T(4,128)S(1)} %get-tuple-element.20, f32[3,256]{1,0:T(4,128)S(1)} %get-tuple-element.21, f32[3,256]{1,0:T(4,128)S(1)} %bitcast.136, ...), kind=kOutput, calls=%fused_computation | convolution fusion | flops 806092800 | bytes 9580544 | tf_op jit(solution)/shard_map/dot_general | solution.py:144
  307.2 1.6 convert_element_type.86
  308.7 1.6 fusion.33
  310.3 5.3 %reduce-scatter.2.cloned.1.call-done = bf16[128,1024]{1,0:T(8,128)(2,1)} async-done(((bf16[128,4096]{1,0:T(8,128)(2,1)}), bf16[128,1024]{1,0:T(8,128)(2,1)}) %reduce-scatter.2.cloned.1.call-update) | async-done | bytes 262160 | tf_op jit(solution)/shard_map/reduce_scatter | solution.py:127
  315.6 1.9 add_convert_fusion
  317.5 65.3 %all-reduce.2.cloned.1.call-done = f32[128,4096]{1,0:T(8,128)} async-done(((f32[128,4096]{1,0:T(8,128)}), f32[128,4096]{1,0:T(8,128)}) %all-reduce.2.cloned.1.call-update) | async-done | bytes 2097168 | tf_op jit(solution)/shard_map/psum | solution.py:145
  382.8 2.1 multiply_reduce_fusion
  384.9 0.1 copy-done.2
  385.0 1.9 subtract_convert_fusion
  (41 shorter events, 0.3 us)
Async XLA Ops:
  7.2 88.3 %all-gather.3.cloned.1.call-start = ((), (), s32[]{:S(2)}) async-start(), calls=%async_computation.3 | async-start | bytes 6389760 | tf_op jit(solution)/shard_map/all_gather | solution.py:89
  7.9 164.4 %all-gather.5.cloned.1.call-start = ((), (), s32[]{:S(2)}) async-start(), calls=%async_computation.4 | async-start | bytes 2129920 | tf_op jit(solution)/shard_map/all_gather | solution.py:90
  11.6 92.6 %copy-start.13 = (f32[128]{0:T(128)}, f32[128]{0:T(128)S(1)}, u32[]{:S(2)}) copy-start(f32[128]{0:T(128)S(1)} %get-tuple-element.19) | copy-start | bytes 1540
  11.6 92.6 %copy-start = (bf16[128,4096]{1,0:T(8,128)(2,1)S(1)}, bf16[128,4096]{1,0:T(8,128)(2,1)}, u32[]{:S(2)}) copy-start(bf16[128,4096]{1,0:T(8,128)(2,1)} %param.8) | copy-start | bytes 3145732
  11.6 92.6 %copy-start.9 = (f32[4096]{0:T(1024)S(1)}, f32[4096]{0:T(1024)}, u32[]{:S(2)}) copy-start(f32[4096]{0:T(1024)} %param.9) | copy-start | bytes 49156
  104.2 68.1 %copy-start.3 = (bf16[128,4096]{1,0:T(8,128)(2,1)S(1)}, bf16[128,4096]{1,0:T(8,128)(2,1)}, u32[]{:S(2)}) copy-start(bf16[128,4096]{1,0:T(8,128)(2,1)} %param.15) | copy-start | bytes 3145732
  109.3 65.4 %collective-permute-start = (bf16[2,3,256]{2,0,1:T(2,128)(2,1)S(1)}, bf16[2,3,256]{2,0,1:T(2,128)(2,1)S(1)}, u32[]{:S(2)}, u32[]{:S(2)}) collective-permute-start(bf16[2,3,256]{2,0,1:T(2,128)(2,1)S(1)} %bitcast.138), channel_id=1, source_target_pairs={{0,4},{4,8},{8,12},{12,16},{16,20},{20,24},{24,28},{28,32},{32,36}... | collective-permute-start | bytes 9224 | tf_op jit(solution)/shard_map/ppermute | solution.py:14
  174.4 1.0 copy-start.7
  174.4 1.0 copy-start.8
  176.4 23.9 %all-to-all-start = ((f32[3,256,128]{2,0,1:T(4,128)}), f32[3,256,128]{2,0,1:T(4,128)S(1)}, u32[]{:S(2)}, u32[]{:S(2)}) async-start(f32[3,256,128]{2,0,1:T(4,128)} %copy.50), calls=%async_computation | async-start | bytes 1048576 | tf_op jit(solution)/shard_map/all_to_all | solution.py:18
  183.0 132.6 %reduce-scatter.2.cloned.1.call-start = ((), (), s32[]{:S(2)}) async-start(), calls=%async_computation.5 | async-start | bytes 1310720 | tf_op jit(solution)/shard_map/reduce_scatter | solution.py:127
  275.9 14.1 %copy-start.11 = (f32[256]{0:T(256)S(1)}, f32[256]{0:T(256)}, u32[]{:S(2)}) copy-start(f32[256]{0:T(256)} %param.13) | copy-start | bytes 3076
  286.0 5.9 %copy-start.1 = (bf16[256,4096]{0,1:T(8,128)(2,1)S(1)}, bf16[256,4096]{0,1:T(8,128)(2,1)}, u32[]{:S(2)}) copy-start(bf16[256,4096]{0,1:T(8,128)(2,1)} %all-gather.5.cloned.1.call-done) | copy-start | bytes 6291460
  293.6 7.0 %copy-start.5 = (f32[128,1,256]{2,0,1:T(8,128)S(1)}, f32[128,1,256]{2,0,1:T(8,128)}, u32[]{:S(2)}) copy-start(f32[128,1,256]{2,0,1:T(8,128)} %get-tuple-element.5) | copy-start | bytes 393220
  293.6 7.0 %copy-start.6 = (f32[128,1,256]{2,0,1:T(8,128)S(1)}, f32[128,1,256]{2,0,1:T(8,128)}, u32[]{:S(2)}) copy-start(f32[128,1,256]{2,0,1:T(8,128)} %get-tuple-element.13) | copy-start | bytes 393220
  293.7 89.1 %all-reduce.2.cloned.1.call-start = ((), (), s32[]{:S(2)}) async-start(), calls=%async_computation.6 | async-start | bytes 4194304 | tf_op jit(solution)/shard_map/psum | solution.py:145
  295.7 4.9 %collective-permute-start.1 = (f32[2,3,256]{2,0,1:T(2,128)S(1)}, f32[2,3,256]{2,0,1:T(2,128)S(1)}, u32[]{:S(2)}, u32[]{:S(2)}) collective-permute-start(f32[2,3,256]{2,0,1:T(2,128)S(1)} %slice.110), channel_id=1, source_target_pairs={{4,0},{8,4},{12,8},{16,12},{20,16},{24,20},{28,24},{32,28},{36,32}... | collective-permute-start | bytes 18440 | tf_op jit(solution)/shard_map/ppermute | solution.py:14
  307.1 75.6 %copy-start.10 = (f32[4096]{0:T(1024)S(1)}, f32[4096]{0:T(1024)}, u32[]{:S(2)}) copy-start(f32[4096]{0:T(1024)} %param.9) | copy-start | bytes 49156
  310.3 74.6 %copy-start.4 = (bf16[128,4096]{1,0:T(8,128)(2,1)S(1)}, bf16[128,4096]{1,0:T(8,128)(2,1)}, u32[]{:S(2)}) copy-start(bf16[128,4096]{1,0:T(8,128)(2,1)} %param.15) | copy-start | bytes 3145732
  310.3 74.6 %copy-start.12 = (f32[128]{0:T(128)S(1)}, f32[128]{0:T(128)}, u32[]{:S(2)}) copy-start(f32[128]{0:T(128)} %get-tuple-element.18) | copy-start | bytes 1540
  310.3 74.6 %copy-start.14 = (f32[128]{0:T(128)S(1)}, f32[128]{0:T(128)}, u32[]{:S(2)}) copy-start(f32[128]{0:T(128)} %copy-done.13) | copy-start | bytes 1540
  382.8 2.2 copy-start.2
Sparse Core Ops, SparseCore 0:
  10.8 84.6 all-gather.2
  98.3 74.0 all-gather.4
  293.8 21.7 reduce-scatter.1
  317.8 64.9 all-reduce.1
where the time goes:
time: 395 us; the launch traced here: 393 us
  waiting for transfers between devices  235 us (59%)
  local copies, waits for them, and re-layouts  62.4 us (16%)
  matrix products  31.7 us (8%)
  blocking collectives  20.6 us (5%)
  other arithmetic  17.5 us (4%)
  between operations  14.1 us (4%)
  starting transfers between devices  12.2 us (3%)
    all_gather x1, waiting for transfers between devices, per_device(): lax.all_gather(in_weight, 'seq', axis=0, tiled=True)  83.9 us
    psum x1, waiting for transfers between devices, per_device(): norm_grad = lax.psum(partial_grad, 'ch')  65.3 us
    all_gather x1, waiting for transfers between devices, per_device(): lax.all_gather(out_weight, 'seq', axis=1, tiled=True)  60.2 us
    unnamed x34, local copies, waits for them, and re-layouts  28.1 us
    all_to_all x1, blocking collectives, to_rows(): lax.all_to_all(signals, 'seq', split_axis=2, concat_axis=1, tiled=True)  20.6 us
    all_to_all x1, waiting for transfers between devices, to_columns(): lax.all_to_all(signals, 'seq', split_axis=1, concat_axis=2, tiled=True)  16.3 us
    all_to_all x4, local copies, waits for them, and re-layouts, to_rows(): lax.all_to_all(signals, 'seq', split_axis=2, concat_axis=1, tiled=True)  14.6 us
    all_gather x1, local copies, waits for them, and re-layouts, per_device(): lax.all_gather(in_weight, 'seq', axis=0, tiled=True)  8.7 us
  transfers between devices with their start and end apart: 7, of which 6 were waited for; matrix products, arithmetic and copies ran while one was open for 8% of the time, Pallas kernels for 0%

commit v1 on v0

--- a/solution.py
+++ b/solution.py
@@ -87,7 +87,9 @@
     normed = (wide_inputs * inv_rms * norm_gain).astype(jnp.bfloat16)
     in_panel, out_panel = (
         lax.all_gather(in_weight, "seq", axis=0, tiled=True),
-        lax.all_gather(out_weight, "seq", axis=1, tiled=True),
+        jnp.concatenate(
+            lax.all_to_all(jnp.stack([out_weight] * lax.axis_size("seq")), "seq", 0, 0), axis=1
+        ),
     )
     in_flat = in_panel.reshape(model_width, 3 * slab_width)
     projected = jnp.dot(normed, in_flat, preferred_element_type=jnp.float32)

time: 395 us -> 353 us (0.89)
  waiting for transfers between devices: 235 us -> 165 us
  starting transfers between devices: 12.2 us -> 27.5 us
  local copies, waits for them, and re-layouts: 62.4 us -> 71.1 us
    all_gather x1 -> x0, waiting for transfers between devices: 60.2 us -> none  [per_device(): lax.all_gather(out_weight, 'seq', axis=1, tiled=True)]
    all_to_all x0 -> x1, starting transfers between devices: none -> 13.1 us  [per_device(): lax.all_to_all(jnp.stack([out_weight] * lax.axis_size('seq')), 'seq', 0, 0)]
    all_gather x1, waiting for transfers between devices: 83.9 us -> 76.3 us  [per_device(): lax.all_gather(in_weight, 'seq', axis=0, tiled=True)]
    all_to_all x1, waiting for transfers between devices: 16.3 us -> 12.1 us  [to_columns(): lax.all_to_all(signals, 'seq', split_axis=1, concat_axis=2, tiled=True)]
    unnamed x34 -> x30, local copies, waits for them, and re-layouts: 28.1 us -> 29.9 us
  transfers between devices with their start and end apart: 7 -> 7, of which waited for: 6 -> 5; matrix products, arithmetic and copies ran while one was open for 8% -> 10% of each run, Pallas kernels for 0% -> 0%
where the time goes in v1:
time: 353 us; the launch traced here: 351 us
  waiting for transfers between devices  165 us (47%)
  local copies, waits for them, and re-layouts  71.1 us (20%)
  matrix products  35.6 us (10%)
  starting transfers between devices  27.5 us (8%)
  blocking collectives  20.9 us (6%)
  other arithmetic  17 us (5%)
  between operations  14.1 us (4%)
    all_gather x1, waiting for transfers between devices, per_device(): lax.all_gather(in_weight, 'seq', axis=0, tiled=True)  76.3 us
    psum x1, waiting for transfers between devices, per_device(): norm_grad = lax.psum(partial_grad, 'ch')  65.5 us
    unnamed x30, local copies, waits for them, and re-layouts  29.9 us
    all_to_all x1, blocking collectives, to_rows(): lax.all_to_all(signals, 'seq', split_axis=2, concat_axis=1, tiled=True)  20.9 us
    all_to_all x4, local copies, waits for them, and re-layouts, to_rows(): lax.all_to_all(signals, 'seq', split_axis=2, concat_axis=1, tiled=True)  14.5 us
    all_to_all x1, starting transfers between devices, per_device(): lax.all_to_all(jnp.stack([out_weight] * lax.axis_size('seq')), 'seq', 0, 0)  13.1 us
    all_to_all x1, waiting for transfers between devices, to_columns(): lax.all_to_all(signals, 'seq', split_axis=1, concat_axis=2, tiled=True)  12.1 us
    div x1, local copies, waits for them, and re-layouts, inverse_dft(): return grid.reshape(count, chans, outer * inner // 2) / float(outer * inner)  9.6 us
  transfers between devices with their start and end apart: 7, of which 5 were waited for; matrix products, arithmetic and copies ran while one was open for 10% of the time, Pallas kernels for 0%

profile of v1, /device:TPU:1, one launch (start us, length us, event | category | flops | bytes accessed | tf_op | source)
XLA Modules:
  0.0 350.8 jit_solution(16134197943182970012)
XLA Ops:
  7.2 0.0 all-gather.2.cloned.1.call-start
  7.2 0.7 all-gather.2.cloned.1.call-update
  7.9 2.4 stack.21
  10.3 13.1 %all-to-all-start = ((bf16[64,256,64]{1,2,0:T(8,128)(2,1)}), bf16[64,256,64]{1,2,0:T(8,128)(2,1)S(1)}, u32[]{:S(2)}, u32[]{:S(2)}) async-start(bf16[64,256,64]{1,2,0:T(8,128)(2,1)} %stack.21), calls=%async_computation | async-start | bytes 4194304 | tf_op jit(solution)/shard_map/all_to_all | solution.py:91
  23.4 0.3 multiply_reduce_fusion.1
  23.7 0.6 multiply_multiply_fusion
  24.3 76.3 %all-gather.2.cloned.1.call-done = bf16[4096,3,256]{2,0,1:T(8,128)(2,1)} async-done(((bf16[64,3,256]{2,0,1:T(8,128)(2,1)}), bf16[4096,3,256]{2,0,1:T(8,128)(2,1)}) %all-gather.2.cloned.1.call-update) | async-done | bytes 6291472 | tf_op jit(solution)/shard_map/all_gather | solution.py:89
  100.6 8.7 %copy.47 = bf16[4096,3,256]{0,2,1:T(8,128)(2,1)} copy(bf16[4096,3,256]{2,0,1:T(8,128)(2,1)} %all-gather.2.cloned.1.call-done) | data formatting | bytes 12582912 | tf_op jit(solution)/shard_map/all_gather | solution.py:89
  109.3 5.0 %convolution_convert_fusion.1 = bf16[128,768]{1,0:T(8,128)(2,1)S(1)} fusion(bf16[4096,768]{0,1:T(8,128)(2,1)} %bitcast.138, bf16[128,4096]{1,0:T(8,128)(2,1)S(1)} %copy-done, f32[4096]{0:T(1024)S(1)} %copy-done.6, f32[128]{0:T(128)S(1)} %get-tuple-element.16), kind=kOutput, calls=%fused_computation.16 | convolution fusion | flops 807501824 | bytes 7553536 | tf_op jit(solution)/shard_map/dot_general | solution.py:95
  114.3 0.6 slice.95
  114.9 2.7 collective-permute-start
  117.6 2.3 fusion.149
  120.0 0.2 copy.49
  120.1 0.2 copy.50
  120.4 0.1 fusion.17
  120.5 0.7 copy-done.4
  121.2 0.0 copy-done.5
  121.2 0.8 maximum_bitcast_fusion
  122.0 2.0 copy.51
  124.0 8.8 %all-to-all-start.1 = ((f32[3,256,128]{2,0,1:T(4,128)}), f32[3,256,128]{2,0,1:T(4,128)}, u32[]{:S(2)}, u32[]{:S(2)}) async-start(f32[3,256,128]{2,0,1:T(4,128)} %copy.51), calls=%async_computation.1 | async-start | bytes 1048576 | tf_op jit(solution)/shard_map/all_to_all | solution.py:18
  132.8 0.2 reduce-scatter.2.cloned.1.call-start
  133.0 0.9 fusion.85
  133.9 1.6 copy.54
  135.5 0.9 fusion.84
  136.4 1.6 copy.55
  137.9 12.1 %all-to-all-done.1 = f32[3,256,128]{2,0,1:T(4,128)} async-done(((f32[3,256,128]{2,0,1:T(4,128)}), f32[3,256,128]{2,0,1:T(4,128)}, u32[]{:S(2)}, u32[]{:S(2)}) %all-to-all-start.1) | async-done | bytes 393248 | tf_op jit(solution)/shard_map/all_to_all | solution.py:18
  150.0 2.6 convolution_bitcast_fusion.1
  152.6 2.5 fusion
  155.1 1.6 fusion.31
  156.7 1.6 fusion.32
  158.3 1.6 convolution_add_fusion.1
  160.0 1.6 convolution_subtract_fusion.1
  161.6 0.1 multiply_add_fusion.3
  161.7 0.1 multiply_subtract_fusion.3
  161.8 1.1 fusion.13
  162.9 1.3 fusion.12
  164.3 1.1 convolution_subtract_fusion
  165.4 1.1 convolution_add_fusion
  166.5 1.2 fusion.8
  167.6 1.9 fusion.2
  169.6 9.6 %copy.86 = f32[3,4,64,128]{1,0,3,2:T(4,128)} copy(f32[3,4,64,128]{3,2,1,0:T(8,128)} %fusion.2) | data formatting | bytes 786432 | tf_op jit(solution)/shard_map/div | solution.py:75
  179.2 16.7 %reshape.122 = f32[64,1,1536]{2,1,0:T(1,128)} reshape(f32[8192,3,4]{2,1,0:T(4,128)} %bitcast.134) | data formatting | bytes 786432
  195.9 20.9 %all_to_all.38 = f32[64,1,1536]{2,1,0:T(1,128)} all-to-all(f32[64,1,1536]{2,1,0:T(1,128)} %reshape.122), channel_id=1, replica_groups=mesh['seq'=64,'ch'=4] {'seq'}, dimensions={0} | all-to-all | bytes 786432 | tf_op jit(solution)/shard_map/all_to_all | solution.py:22
  216.8 0.5 broadcast.228
  217.3 3.3 reduce
  220.7 12.4 %reshape.123 = f32[8192,3,4]{2,1,0:T(4,128)} reshape(f32[64,1536]{1,0:T(8,128)} %reduce) | data formatting | bytes 786432
  233.0 10.1 %copy.87 = f32[3,4,64,128]{3,2,1,0:T(8,128)} copy(f32[3,4,64,128]{1,0,3,2:T(4,128)} %bitcast.135) | data formatting | bytes 786432 | tf_op jit(solution)/shard_map/all_to_all | solution.py:22
  243.1 2.0 copy.68
  245.1 1.9 copy.69
  247.0 2.7 convolution_convert_fusion
  249.7 0.0 reduce-scatter.2.cloned.1.call-update
  249.7 0.0 all-reduce.2.cloned.1.call-start
  249.8 1.1 fusion.39
  250.9 2.6 collective-permute-start.1
  253.5 2.4 collective-permute-done.1
  255.9 6.3 %convolution_bitcast_fusion = f32[128,4096]{1,0:T(8,128)} fusion(bf16[4096,3,256]{2,0,1:T(8,128)(2,1)} %all-gather.2.cloned.1.call-done, f32[130,3,256]{2,0,1:T(8,128)S(1)} %pad_maximum_fusion.6, f32[3,256]{1,0:T(4,128)S(1)} %get-tuple-element.17, f32[3,256]{1,0:T(4,128)S(1)} %get-tuple-element.18, f32[3,256]{1,0:T(4,128)S(1)} %bitcast.146, ...), kind=kOutput, calls=%fused_computation | convolution fusion | flops 806092800 | bytes 9580544 | tf_op jit(solution)/shard_map/dot_general | solution.py:146
  262.3 0.2 convert_element_type.89
  262.5 1.6 fusion.33
  264.1 7.7 %reduce-scatter.2.cloned.1.call-done = bf16[128,1024]{1,0:T(8,128)(2,1)} async-done(((bf16[128,4096]{1,0:T(8,128)(2,1)}), bf16[128,1024]{1,0:T(8,128)(2,1)}) %reduce-scatter.2.cloned.1.call-update) | async-done | bytes 262160 | tf_op jit(solution)/shard_map/reduce_scatter | solution.py:129
  271.7 1.7 add_convert_fusion
  273.4 65.5 %all-reduce.2.cloned.1.call-done = f32[128,4096]{1,0:T(8,128)} async-done(((f32[128,4096]{1,0:T(8,128)}), f32[128,4096]{1,0:T(8,128)}) %all-reduce.2.cloned.1.call-update) | async-done | bytes 2097168 | tf_op jit(solution)/shard_map/psum | solution.py:147
  339.0 2.1 multiply_reduce_fusion
  341.1 0.1 copy-done.1
  341.2 3.1 subtract_convert_fusion
  (37 shorter events, 0.3 us)
Async XLA Ops:
  7.2 93.4 %all-gather.2.cloned.1.call-start = ((), (), s32[]{:S(2)}) async-start(), calls=%async_computation.4 | async-start | bytes 6389760 | tf_op jit(solution)/shard_map/all_gather | solution.py:89
  10.3 13.1 %copy-start.8 = (f32[3,3,256]{2,1,0:T(4,128)S(1)}, f32[3,3,256]{2,1,0:T(4,128)}, u32[]{:S(2)}) copy-start(f32[3,3,256]{2,1,0:T(4,128)} %param.11) | copy-start | bytes 27652
  10.3 13.2 %copy-start = (bf16[128,4096]{1,0:T(8,128)(2,1)S(1)}, bf16[128,4096]{1,0:T(8,128)(2,1)}, u32[]{:S(2)}) copy-start(bf16[128,4096]{1,0:T(8,128)(2,1)} %param.8) | copy-start | bytes 3145732
  10.3 107.3 %all-to-all-start = ((bf16[64,256,64]{1,2,0:T(8,128)(2,1)}), bf16[64,256,64]{1,2,0:T(8,128)(2,1)S(1)}, u32[]{:S(2)}, u32[]{:S(2)}) async-start(bf16[64,256,64]{1,2,0:T(8,128)(2,1)} %stack.21), calls=%async_computation | async-start | bytes 4194304 | tf_op jit(solution)/shard_map/all_to_all | solution.py:91
  24.3 85.0 %copy-start.11 = (f32[128]{0:T(128)}, f32[128]{0:T(128)S(1)}, u32[]{:S(2)}) copy-start(f32[128]{0:T(128)S(1)} %get-tuple-element.16) | copy-start | bytes 1540
  24.3 85.0 %copy-start.6 = (f32[4096]{0:T(1024)S(1)}, f32[4096]{0:T(1024)}, u32[]{:S(2)}) copy-start(f32[4096]{0:T(1024)} %param.9) | copy-start | bytes 49156
  114.9 5.4 %collective-permute-start = (bf16[2,3,256]{2,0,1:T(2,128)(2,1)}, bf16[2,3,256]{2,0,1:T(2,128)(2,1)S(1)}, u32[]{:S(2)}, u32[]{:S(2)}) collective-permute-start(bf16[2,3,256]{2,0,1:T(2,128)(2,1)} %bitcast.1), channel_id=1, source_target_pairs={{0,4},{4,8},{8,12},{12,16},{16,20},{20,24},{24,28},{28,32},{32,36}... | collective-permute-start | bytes 9224 | tf_op jit(solution)/shard_map/ppermute | solution.py:14
  120.3 0.9 copy-start.4
  120.3 1.0 copy-start.5
  124.0 26.0 %all-to-all-start.1 = ((f32[3,256,128]{2,0,1:T(4,128)}), f32[3,256,128]{2,0,1:T(4,128)}, u32[]{:S(2)}, u32[]{:S(2)}) async-start(f32[3,256,128]{2,0,1:T(4,128)} %copy.51), calls=%async_computation.1 | async-start | bytes 1048576 | tf_op jit(solution)/shard_map/all_to_all | solution.py:18
  132.8 138.9 %reduce-scatter.2.cloned.1.call-start = ((), (), s32[]{:S(2)}) async-start(), calls=%async_computation.5 | async-start | bytes 1310720 | tf_op jit(solution)/shard_map/reduce_scatter | solution.py:129
  150.0 5.1 %copy-start.2 = (f32[128,128]{0,1:T(8,128)S(1)}, f32[128,128]{0,1:T(8,128)}, u32[]{:S(2)}) copy-start(f32[128,128]{0,1:T(8,128)} %copy.54) | copy-start | bytes 196612
  150.0 5.1 %copy-start.3 = (f32[128,128]{0,1:T(8,128)S(1)}, f32[128,128]{0,1:T(8,128)}, u32[]{:S(2)}) copy-start(f32[128,128]{0,1:T(8,128)} %copy.55) | copy-start | bytes 196612
  233.0 14.0 %copy-start.9 = (f32[256]{0:T(256)S(1)}, f32[256]{0:T(256)}, u32[]{:S(2)}) copy-start(f32[256]{0:T(256)} %param.13) | copy-start | bytes 3076
  249.7 89.3 %all-reduce.2.cloned.1.call-start = ((), (), s32[]{:S(2)}) async-start(), calls=%async_computation.6 | async-start | bytes 4194304 | tf_op jit(solution)/shard_map/psum | solution.py:147
  250.9 4.9 %collective-permute-start.1 = (f32[2,3,256]{2,0,1:T(2,128)S(1)}, f32[2,3,256]{2,0,1:T(2,128)S(1)}, u32[]{:S(2)}, u32[]{:S(2)}) collective-permute-start(f32[2,3,256]{2,0,1:T(2,128)S(1)} %slice.110), channel_id=1, source_target_pairs={{4,0},{8,4},{12,8},{16,12},{20,16},{24,20},{28,24},{32,28},{36,32}... | collective-permute-start | bytes 18440 | tf_op jit(solution)/shard_map/ppermute | solution.py:14
  262.3 76.7 %copy-start.7 = (f32[4096]{0:T(1024)S(1)}, f32[4096]{0:T(1024)}, u32[]{:S(2)}) copy-start(f32[4096]{0:T(1024)} %param.9) | copy-start | bytes 49156
  264.1 77.0 %copy-start.10 = (f32[128]{0:T(128)S(1)}, f32[128]{0:T(128)}, u32[]{:S(2)}) copy-start(f32[128]{0:T(128)} %get-tuple-element.15) | copy-start | bytes 1540
  264.1 77.0 %copy-start.12 = (f32[128]{0:T(128)S(1)}, f32[128]{0:T(128)}, u32[]{:S(2)}) copy-start(f32[128]{0:T(128)} %copy-done.11) | copy-start | bytes 1540
  339.0 2.2 copy-start.1
Sparse Core Ops, SparseCore 0:
  10.8 89.7 all-gather.1
  249.8 21.8 reduce-scatter.1
  274.1 64.8 all-reduce.1
